TPU v7x, 128 devices: a whole 4x4x4 slice. The times are simulated.
128 devices in a mesh: pr: 8 (over z, core), pc: 16 (over y, x).
Axes of the slice: x: 4, y: 4, z: 4, core: 2. Of those that a mesh axis runs over, the one named last changes fastest.
Arguments:
- test_points: bfloat16 [131072, 512], P('pr'), may hold values from -15 to 15
- panel_points: bfloat16 [1024, 512], P('pc'), may hold values from -15 to 15
- factor_rows: float32 [1024, 32768], P('pc', 'pr'), may hold values from -0.03125 to 0.03125
- alpha_below: float32 [32768, 128], P(('pr', 'pc')), may hold values from -6 to 6
- targets: float32 [1024, 128], P('pc'), may hold values from -6 to 6
- inverse_block: float32 [1024, 1024], P('pc'), may hold values from -0.008 to 0.08, as said below
- predictions_in: float32 [131072, 128], P(('pr', 'pc')), may hold values from -6 to 6
Outputs:
- predictions: float32 [131072, 128], P(('pr', 'pc'))
Inputs may be any that keep to these rules, and one draw needn't show every extreme that they name: `inverse_block`: lower triangular with a positive diagonal.
All inputs are finite; a program needn't handle non-finite values.
Results may differ from a plain program's by a relative error of at most 0.0003.
Values may be sent and summed in bfloat16 or wider, within the bound.
No kernel may reach another device: no remote copies, remote signals or barrier semaphores. Data moves between devices by JAX's collectives and lax.ppermute only.
A program may use at most 128 MiB of HBM per device.

v0:
```python
import math
import jax
import jax.numpy as jnp
from jax import lax
from jax.sharding import PartitionSpec as P

LAYERS = 4
bias_var = 0.1
weight_var = 2.0


def arc_kernel(panel, test, test_norms):
    width = panel.shape[1]
    cross = jnp.dot(panel, test.T, preferred_element_type=jnp.float32) / width
    panel_var = jnp.einsum("pd,pd->p", panel, panel, preferred_element_type=jnp.float32) / width
    kern = bias_var + weight_var * cross
    panel_k = bias_var + weight_var * panel_var
    test_k = bias_var + weight_var * (test_norms / width)
    for level in range(LAYERS):
        spread = jnp.sqrt(panel_k[:, None] * test_k[None, :])
        cosine = kern / spread
        theta = jnp.arccos(cosine)
        kern = bias_var + weight_var / (2.0 * math.pi) * spread * (
            jnp.sqrt(1.0 - cosine * cosine) + (math.pi - theta) * cosine
        )
        panel_k = bias_var + 0.5 * weight_var * panel_k
        test_k = bias_var + 0.5 * weight_var * test_k
    return kern


def contract_rows(left, right):
    return lax.dot_general(
        left,
        right,
        (((0,), (0,)), ((), ())),
        precision=lax.Precision.HIGHEST,
        preferred_element_type=jnp.float32,
    )


def body(
    test_points, panel_points, factor_rows, alpha_below, targets, inverse_block, predictions_in
):
    rows = predictions_in.shape[0]
    own = lax.axis_index("pc")
    partial_sum = jnp.dot(
        factor_rows,
        lax.all_gather(alpha_below, "pc", axis=0, tiled=True),
        precision=lax.Precision.HIGHEST,
        preferred_element_type=jnp.float32,
    )
    carried = lax.psum(partial_sum, "pr")
    residual = targets - carried
    alpha_panel = lax.psum(contract_rows(inverse_block, residual), "pc")
    panel_all = lax.all_gather(panel_points, "pc", axis=0, tiled=True)
    test_own = lax.dynamic_slice_in_dim(test_points, own * rows, rows, 0)
    test_norms = jnp.einsum("nd,nd->n", test_own, test_own, preferred_element_type=jnp.float32)
    kern = lax.optimization_barrier(arc_kernel(panel_all, test_own, test_norms))
    update = contract_rows(kern, alpha_panel)
    return predictions_in + update


def solution(mesh):
    placed = (
        P("pr", None),
        P("pc", None),
        P("pc", "pr"),
        P(("pr", "pc"), None),
        P("pc", None),
        P("pc", None),
        P(("pr", "pc"), None),
    )
    return jax.shard_map(
        body, mesh=mesh, in_specs=placed, out_specs=P(("pr", "pc"), None), check_vma=False
    )
```

profile of v0, /device:TPU:0, one launch (start us, length us, event | category | flops | bytes accessed | tf_op | source)
XLA Modules:
  0.0 224.8 jit_solution(2418785735525503081)
XLA Ops:
  6.5 0.0 copy-start
  6.5 0.0 copy-start.3
  6.5 0.0 copy-start.4
  6.5 0.0 all-gather.3.cloned.1.call-start
  6.5 0.7 all-gather.3.cloned.1.call-update
  7.3 0.0 all-gather.5.cloned.1.call-start
  7.3 0.7 all-gather.5.cloned.1.call-update
  8.0 0.0 all-reduce.2.cloned.1.call-start
  8.1 1.5 fusion
  9.6 44.7 %all-gather.3.cloned.1.call-done = bf16[1024,512]{1,0:T(8,128)(2,1)} async-done(((bf16[64,512]{1,0:T(8,128)(2,1)}), bf16[1024,512]{1,0:T(8,128)(2,1)}) %all-gather.3.cloned.1.call-update) | async-done | bytes 1048592 | tf_op jit(solution)/shard_map/all_gather | solution.py:55
  54.3 0.0 copy-start.1
  54.3 1.6 fusion.1
  55.9 44.7 %all-gather.5.cloned.1.call-done = f32[4096,128]{1,0:T(8,128)} async-done(((f32[256,128]{1,0:T(8,128)}), f32[4096,128]{1,0:T(8,128)}) %all-gather.5.cloned.1.call-update) | async-done | bytes 2097168 | tf_op jit(solution)/shard_map/all_gather | solution.py:48
  100.6 0.0 copy-done
  100.6 3.0 %fusion.5 = f32[64,128]{1,0:T(8,128)S(1)} fusion(f32[64,4096]{1,0:T(8,128)S(1)} %copy-done, f32[4096,128]{1,0:T(8,128)} %all-gather.5.cloned.1.call-done), kind=kOutput, calls=%fused_computation.19 | convolution fusion | flops 402653184 | bytes 3178496 | tf_op jit(solution)/shard_map/dot_general | solution.py:46
  103.6 24.3 %psum.14 = f32[64,128]{1,0:T(8,128)S(1)} all-reduce(f32[64,128]{1,0:T(8,128)S(1)} %fusion.5), channel_id=1, replica_groups=mesh['pr'=8,'pc'=16] {'pr'}, use_global_device_ids=true, to_apply=%region_0.0 | all-reduce | flops 8192 | bytes 65536 | tf_op jit(solution)/shard_map/psum | solution.py:52
  127.9 0.0 copy-done.3
  127.9 0.0 copy-done.4
  127.9 1.4 convolution_bitcast_fusion
  129.3 0.0 all-reduce.2.cloned.1.call-update
  129.3 0.0 copy-done.1
  129.4 0.0 copy-start.2
  129.4 50.0 %multiply_add_fusion = f32[1024,1024]{0,1:T(8,128)} fusion(bf16[1024,512]{1,0:T(8,128)(2,1)S(1)} %copy-done.1, f32[1024]{0:T(1024)S(1)} %get-tuple-element.12, f32[1024]{0:T(1024)S(1)} %get-tuple-element.8, f32[1024]{0:T(1024)S(1)} %get-tuple-element.11, f32[1024]{0:T(1024)S(1)} %get-tuple-element.7, f32[1024]{0:T(1024)S(1)} %get-tuple-element.10, ...), kind=kOutput, calls=%fused_computation.1 | convolution fusion | flops 1130364928 | bytes 6324228 | tf_op jit(solution)/shard_map/dot_general | solution.py:14
  179.3 32.4 %all-reduce.2.cloned.1.call-done = f32[1024,128]{0,1:T(8,128)} async-done(((f32[1024,128]{0,1:T(8,128)}), f32[1024,128]{0,1:T(8,128)}) %all-reduce.2.cloned.1.call-update) | async-done | bytes 524304 | tf_op jit(solution)/shard_map/psum | solution.py:54
  211.7 0.0 copy-done.2
  211.7 6.5 %convolution_add_fusion = f32[1024,128]{1,0:T(8,128)} fusion(f32[1024,128]{1,0:T(8,128)S(1)} %copy-done.2, f32[1024,1024]{0,1:T(8,128)} %multiply_add_fusion, f32[1024,128]{0,1:T(8,128)} %all-reduce.2.cloned.1.call-done), kind=kOutput, calls=%fused_computation.6 | convolution fusion | flops 1610743808 | bytes 5767168 | tf_op jit(solution)/shard_map/dot_general | solution.py:32
  (2 shorter events, 0.0 us)
Async XLA Ops:
  6.5 94.1 %copy-start = (f32[64,4096]{1,0:T(8,128)S(1)}, f32[64,4096]{1,0:T(8,128)}, u32[]{:S(2)}) copy-start(f32[64,4096]{1,0:T(8,128)} %param.9) | copy-start | bytes 3145732
  6.5 121.4 %copy-start.3 = (f32[64,1024]{1,0:T(8,128)S(1)}, f32[64,1024]{1,0:T(8,128)}, u32[]{:S(2)}) copy-start(f32[64,1024]{1,0:T(8,128)} %param.12) | copy-start | bytes 786436
  6.5 121.4 %copy-start.4 = (f32[64,128]{1,0:T(8,128)S(1)}, f32[64,128]{1,0:T(8,128)}, u32[]{:S(2)}) copy-start(f32[64,128]{1,0:T(8,128)} %param.11) | copy-start | bytes 98308
  6.5 47.8 %all-gather.3.cloned.1.call-start = ((), (), s32[]{:S(2)}) async-start(), calls=%async_computation | async-start | bytes 1114112 | tf_op jit(solution)/shard_map/all_gather | solution.py:55
  7.3 93.4 %all-gather.5.cloned.1.call-start = ((), (), s32[]{:S(2)}) async-start(), calls=%async_computation.1 | async-start | bytes 2228224 | tf_op jit(solution)/shard_map/all_gather | solution.py:48
  8.0 203.7 %all-reduce.2.cloned.1.call-start = ((), (), s32[]{:S(2)}) async-start(), calls=%async_computation.2 | async-start | bytes 1048576 | tf_op jit(solution)/shard_map/psum | solution.py:54
  54.3 75.0 %copy-start.1 = (bf16[1024,512]{1,0:T(8,128)(2,1)S(1)}, bf16[1024,512]{1,0:T(8,128)(2,1)}, u32[]{:S(2)}) copy-start(bf16[1024,512]{1,0:T(8,128)(2,1)} %all-gather.3.cloned.1.call-done) | copy-start | bytes 3145732
  129.4 82.4 %copy-start.2 = (f32[1024,128]{1,0:T(8,128)S(1)}, f32[1024,128]{1,0:T(8,128)}, u32[]{:S(2)}) copy-start(f32[1024,128]{1,0:T(8,128)} %param.13) | copy-start | bytes 1572868
Sparse Core Ops, SparseCore 0:
  9.5 44.8 all-gather.2
  56.5 44.1 all-gather.4
  129.5 82.2 all-reduce.1
where the time goes:
time: 225 us
  waiting for transfers between devices  123 us (55%)
  matrix products  60.9 us (27%)
  blocking collectives  24.3 us (11%)
  between operations  13.2 us (6%)
  other arithmetic  3.1 us (1%)
    dot_general x1, matrix products, arc_kernel(): cross = jnp.dot(panel, test.T, preferred_element_type=jnp.float32) / width  50 us
    all_gather x1, waiting for transfers between devices, body(): panel_all = lax.all_gather(panel_points, 'pc', axis=0, tiled=True)  44.7 us
    all_gather x1, waiting for transfers between devices, body(): lax.all_gather(alpha_below, 'pc', axis=0, tiled=True)  44.7 us
    psum x1, waiting for transfers between devices, body(): alpha_panel = lax.psum(contract_rows(inverse_block, residual), 'pc')  32.4 us
    psum x1, blocking collectives, body(): carried = lax.psum(partial_sum, 'pr')  24.3 us
    dot_general x2, matrix products, contract_rows(): lax.dot_general(left, right, (((0,), (0,)), ((), ())), precision=lax.Prec...  7.94 us
  transfers between devices with their start and end apart: 3, of which 3 were waited for; matrix products, arithmetic and copies ran while one was open for 24% of the time, Pallas kernels for 0%

commit v1 on v0

--- a/solution.py
+++ b/solution.py
@@ -45,7 +45,9 @@
     own = lax.axis_index("pc")
     partial_sum = jnp.dot(
         factor_rows,
-        lax.all_gather(alpha_below, "pc", axis=0, tiled=True),
+        jnp.concatenate(
+            lax.all_to_all(jnp.stack([alpha_below] * lax.axis_size("pc")), "pc", 0, 0), axis=0
+        ),
         precision=lax.Precision.HIGHEST,
         preferred_element_type=jnp.float32,
     )

time: 225 us -> 191 us (0.85)
  waiting for transfers between devices: 123 us -> 81.1 us
  starting transfers between devices: 0.08 us -> 7.32 us
  local copies, waits for them, and re-layouts: 0.02 us -> 2.46 us
    all_gather x1 -> x0, waiting for transfers between devices: 44.7 us -> none  [body(): lax.all_gather(alpha_below, 'pc', axis=0, tiled=True)]
    all_to_all x0 -> x1, starting transfers between devices: none -> 7.28 us  [body(): lax.all_to_all(jnp.stack([alpha_below] * lax.axis_size('pc')), 'pc', 0, 0)]
    all_gather x1, waiting for transfers between devices: 44.7 us -> 48.6 us  [body(): panel_all = lax.all_gather(panel_points, 'pc', axis=0, tiled=True)]
    another operation x0 -> x1, local copies, waits for them, and re-layouts: none -> 2.44 us  [body(): jnp.stack([alpha_below] * lax.axis_size('pc'))]
  transfers between devices with their start and end apart: 3 -> 3, of which waited for: 3 -> 2; matrix products, arithmetic and copies ran while one was open for 24% -> 29% of each run, Pallas kernels for 0% -> 0%
where the time goes in v1:
time: 191 us
  waiting for transfers between devices  81.1 us (42%)
  matrix products  59.7 us (31%)
  blocking collectives  24 us (13%)
  between operations  13.5 us (7%)
  starting transfers between devices  7.32 us (4%)
  other arithmetic  3.01 us (2%)
  local copies, waits for them, and re-layouts  2.46 us (1%)
    dot_general x1, matrix products, arc_kernel(): cross = jnp.dot(panel, test.T, preferred_element_type=jnp.float32) / width  50.3 us
    all_gather x1, waiting for transfers between devices, body(): panel_all = lax.all_gather(panel_points, 'pc', axis=0, tiled=True)  48.6 us
    psum x1, waiting for transfers between devices, body(): alpha_panel = lax.psum(contract_rows(inverse_block, residual), 'pc')  31.7 us
    psum x1, blocking collectives, body(): carried = lax.psum(partial_sum, 'pr')  24 us
    dot_general x2, matrix products, contract_rows(): lax.dot_general(left, right, (((0,), (0,)), ((), ())), precision=lax.Prec...  7.94 us
    all_to_all x1, starting transfers between devices, body(): lax.all_to_all(jnp.stack([alpha_below] * lax.axis_size('pc')), 'pc', 0, 0)  7.28 us
  transfers between devices with their start and end apart: 3, of which 2 were waited for; matrix products, arithmetic and copies ran while one was open for 29% of the time, Pallas kernels for 0%

profile of v1, /device:TPU:0, one launch (start us, length us, event | category | flops | bytes accessed | tf_op | source)
XLA Modules:
  0.0 191.1 jit_solution(10434228050600634698)
XLA Ops:
  6.5 0.0 copy-start
  6.5 0.0 all-gather.2.cloned.1.call-start
  6.5 0.7 all-gather.2.cloned.1.call-update
  7.3 2.4 %stack.2 = f32[16,256,128]{2,1,0:T(8,128)} broadcast(f32[256,128]{1,0:T(8,128)} %param.10), dimensions={1,2} | broadcast | bytes 2228224 | tf_op jit(solution)/shard_map/stack | solution.py:49
  9.7 0.0 copy-start.2
  9.7 0.0 copy-start.3
  9.7 7.3 %all-to-all-start = ((f32[16,256,128]{2,1,0:T(8,128)}), f32[16,256,128]{2,1,0:T(8,128)S(1)}, u32[]{:S(2)}, u32[]{:S(2)}) async-start(f32[16,256,128]{2,1,0:T(8,128)} %stack.2), calls=%async_computation | async-start | bytes 4194304 | tf_op jit(solution)/shard_map/all_to_all | solution.py:49
  17.0 0.0 all-reduce.2.cloned.1.call-start
  17.0 1.5 fusion
  18.6 48.6 %all-gather.2.cloned.1.call-done = bf16[1024,512]{1,0:T(8,128)(2,1)} async-done(((bf16[64,512]{1,0:T(8,128)(2,1)}), bf16[1024,512]{1,0:T(8,128)(2,1)}) %all-gather.2.cloned.1.call-update) | async-done | bytes 1048592 | tf_op jit(solution)/shard_map/all_gather | solution.py:57
  67.2 1.5 fusion.1
  68.7 0.0 all-to-all-done
  68.7 0.0 copy-done
  68.7 1.4 fusion.5
  70.1 24.0 %psum.14 = f32[64,128]{1,0:T(8,128)S(1)} all-reduce(f32[64,128]{1,0:T(8,128)S(1)} %fusion.5), channel_id=1, replica_groups=mesh['pr'=8,'pc'=16] {'pr'}, use_global_device_ids=true, to_apply=%region_0.0 | all-reduce | flops 8192 | bytes 65536 | tf_op jit(solution)/shard_map/psum | solution.py:54
  94.1 0.0 copy-done.2
  94.2 0.0 copy-done.3
  94.2 1.4 convolution_bitcast_fusion
  95.6 0.0 all-reduce.2.cloned.1.call-update
  95.6 0.0 copy-start.1
  95.6 50.3 %multiply_add_fusion = f32[1024,1024]{0,1:T(8,128)} fusion(bf16[1024,512]{1,0:T(8,128)(2,1)} %all-gather.2.cloned.1.call-done, f32[1024]{0:T(1024)S(1)} %get-tuple-element.12, f32[1024]{0:T(1024)S(1)} %get-tuple-element.8, f32[1024]{0:T(1024)S(1)} %get-tuple-element.11, f32[1024]{0:T(1024)S(1)} %get-tuple-element.7, f32[1024]{0:T(1024)S(1)} %get-tuple-element.10, ...), kind=kOutput, calls=%fused_computation.1 | convolution fusion | flops 1130364928 | bytes 6324228 | tf_op jit(solution)/shard_map/dot_general | solution.py:14
  145.9 31.7 %all-reduce.2.cloned.1.call-done = f32[1024,128]{0,1:T(8,128)} async-done(((f32[1024,128]{0,1:T(8,128)}), f32[1024,128]{0,1:T(8,128)}) %all-reduce.2.cloned.1.call-update) | async-done | bytes 524304 | tf_op jit(solution)/shard_map/psum | solution.py:56
  177.7 0.0 copy-done.1
  177.7 6.5 %convolution_add_fusion = f32[1024,128]{1,0:T(8,128)} fusion(f32[1024,128]{1,0:T(8,128)S(1)} %copy-done.1, f32[1024,1024]{0,1:T(8,128)} %multiply_add_fusion, f32[1024,128]{0,1:T(8,128)} %all-reduce.2.cloned.1.call-done), kind=kOutput, calls=%fused_computation.6 | convolution fusion | flops 1610743808 | bytes 5767168 | tf_op jit(solution)/shard_map/dot_general | solution.py:32
  (2 shorter events, 0.0 us)
Async XLA Ops:
  6.5 62.2 %copy-start = (f32[64,4096]{1,0:T(8,128)S(1)}, f32[64,4096]{1,0:T(8,128)}, u32[]{:S(2)}) copy-start(f32[64,4096]{1,0:T(8,128)} %param.9) | copy-start | bytes 3145732
  6.5 60.6 %all-gather.2.cloned.1.call-start = ((), (), s32[]{:S(2)}) async-start(), calls=%async_computation.1 | async-start | bytes 1114112 | tf_op jit(solution)/shard_map/all_gather | solution.py:57
  9.7 84.4 %copy-start.2 = (f32[64,1024]{1,0:T(8,128)S(1)}, f32[64,1024]{1,0:T(8,128)}, u32[]{:S(2)}) copy-start(f32[64,1024]{1,0:T(8,128)} %param.12) | copy-start | bytes 786436
  9.7 84.4 %copy-start.3 = (f32[64,128]{1,0:T(8,128)S(1)}, f32[64,128]{1,0:T(8,128)}, u32[]{:S(2)}) copy-start(f32[64,128]{1,0:T(8,128)} %param.11) | copy-start | bytes 98308
  9.7 59.0 %all-to-all-start = ((f32[16,256,128]{2,1,0:T(8,128)}), f32[16,256,128]{2,1,0:T(8,128)S(1)}, u32[]{:S(2)}, u32[]{:S(2)}) async-start(f32[16,256,128]{2,1,0:T(8,128)} %stack.2), calls=%async_computation | async-start | bytes 4194304 | tf_op jit(solution)/shard_map/all_to_all | solution.py:49
  17.0 160.7 %all-reduce.2.cloned.1.call-start = ((), (), s32[]{:S(2)}) async-start(), calls=%async_computation.2 | async-start | bytes 1048576 | tf_op jit(solution)/shard_map/psum | solution.py:56
  95.6 82.1 %copy-start.1 = (f32[1024,128]{1,0:T(8,128)S(1)}, f32[1024,128]{1,0:T(8,128)}, u32[]{:S(2)}) copy-start(f32[1024,128]{1,0:T(8,128)} %param.13) | copy-start | bytes 1572868
Sparse Core Ops, SparseCore 0:
  9.5 57.6 all-gather.1
  95.7 81.9 all-reduce.1
